TPU v7x, 512 devices: a whole 4x4x16 slice. The times are simulated.
512 devices in a mesh: dp: 64 (over y, z), tensor: 8 (over x, core).
Axes of the slice: x: 4, y: 4, z: 16, core: 2. Of those that a mesh axis runs over, the one named last changes fastest.
Arguments:
- tokens: bfloat16 [65536, 1408], P(('dp', 'tensor')), may hold values from -6 to 6
- ln1_gain: float32 [1408], replicated, may hold values from 0.1 to 1.9
- ln1_shift: float32 [1408], replicated, may hold values from -3 to 3
- w_qkv: bfloat16 [1408, 16, 264], P(None, 'tensor')
- w_out: bfloat16 [16, 88, 1408], P('tensor'), may hold values from -0.625 to 0.625
- ln2_gain: float32 [1408], replicated, may hold values from 0.1 to 1.9
- ln2_shift: float32 [1408], replicated, may hold values from -3 to 3
- w_proj: bfloat16 [5632, 3584], P('dp', 'tensor'), may hold values from -0.078125 to 0.078125
- proj_bias: float32 [3584], P('tensor'), may hold values from -3 to 3
- segments: int32 [64, 256], P('dp'), may hold values from 0 to 7, never falling along the last dimension, each value on 1 to 128 neighbouring positions
- owners: int32 [16384, 1], P('dp'), may hold values from 0 to 63; in each aligned block of 256 rows (0 to 255, 256 to 511, ...) at most 8 rows name the same one
Outputs:
- delivered: bfloat16 [32768, 3584], P('dp', 'tensor')
Inputs may be any that keep to these rules, and one draw needn't show every extreme that they name: `segments`: within a pack numbers never fall, every image has 1 to 128 groups and one has exactly that many. `owners`: among the 256 merged tokens of one pack no owner gets more than 8; in some pack an owner gets exactly 8.
All inputs are finite; a program needn't handle non-finite values.
Results may differ from a plain program's by a relative error of at most 0.015.
Values may be sent and summed in bfloat16 or wider, within the bound.
No kernel may reach another device: no remote copies, remote signals or barrier semaphores. Data moves between devices by JAX's collectives and lax.ppermute only.
A program may use at most 64 MiB of HBM per device.

v0:
```python
import jax
import jax.numpy as jnp
from jax import lax
from jax.sharding import PartitionSpec as P


def layer_norm(values, gain, shift):
    wide = values.astype(jnp.float32)
    average = jnp.mean(wide, axis=-1, keepdims=True)
    centred = wide - average
    variance = jnp.mean(centred * centred, axis=-1, keepdims=True)
    return centred * lax.rsqrt(variance + 1e-06) * gain + shift


def attend(heads_qkv, token_segs):
    row_count = heads_qkv.shape[0]
    width = heads_qkv.shape[2] // 3
    queries = heads_qkv[:, :, :width]
    keys_all = heads_qkv[:, :, width : 2 * width]
    values_all = heads_qkv[:, :, 2 * width :]
    score_scale = 1.0 / jnp.sqrt(jnp.float32(width))
    block_rows = min(512, row_count)
    outputs = []
    for block_index in range(row_count // block_rows):
        lower = block_index * block_rows
        scores = (
            jnp.einsum(
                "qhd,khd->hqk",
                queries[lower : lower + block_rows],
                keys_all,
                preferred_element_type=jnp.float32,
            )
            * score_scale
        )
        same = token_segs[lower : lower + block_rows][:, None] == token_segs[None, :]
        scores = jnp.where(same[None], scores, -jnp.inf)
        row_max = jnp.max(scores, axis=-1, keepdims=True)
        exponent = jnp.exp(scores - row_max)
        probs = (exponent / jnp.sum(exponent, axis=-1, keepdims=True)).astype(jnp.bfloat16)
        context = jnp.einsum("hqk,khd->qhd", probs, values_all, preferred_element_type=jnp.float32)
        outputs.append(context.astype(jnp.bfloat16))
    return jnp.concatenate(outputs, axis=0)


def shards(
    tokens,
    ln1_gain,
    ln1_shift,
    w_qkv,
    w_out,
    ln2_gain,
    ln2_shift,
    w_proj,
    proj_bias,
    segments,
    owners,
):
    dp_count = lax.axis_size("dp")
    gathered = lax.all_gather(tokens, "tensor", axis=0, tiled=True)
    row_count = gathered.shape[0]
    normed = layer_norm(gathered, ln1_gain, ln1_shift).astype(jnp.bfloat16)
    heads_here = w_qkv.shape[1]
    heads_qkv = jnp.dot(
        normed, w_qkv.reshape(w_qkv.shape[0], -1), preferred_element_type=jnp.float32
    )
    heads_qkv = heads_qkv.astype(jnp.bfloat16).reshape(row_count, heads_here, -1)
    token_segs = jnp.repeat(segments[0], 4)
    context = attend(heads_qkv, token_segs).reshape(row_count, -1)
    out_flat = w_out.reshape(-1, w_out.shape[2])
    attn_all = lax.psum(
        jnp.dot(context, out_flat, preferred_element_type=jnp.float32).astype(jnp.bfloat16),
        "tensor",
    ).astype(jnp.float32)
    hidden = (gathered.astype(jnp.float32) + attn_all).astype(jnp.bfloat16)
    normed_all = layer_norm(hidden, ln2_gain, ln2_shift).astype(jnp.bfloat16)
    groups = row_count // 4
    merged = normed_all.reshape(groups, -1)
    summed = jnp.dot(
        merged, lax.all_gather(w_proj, "dp", axis=0, tiled=True), preferred_element_type=jnp.float32
    )
    projected = (summed + proj_bias).astype(jnp.bfloat16)
    dests = owners[:, 0]
    onehot = (dests[:, None] == jnp.arange(dp_count, dtype=jnp.int32)[None, :]).astype(jnp.int32)
    earlier = jnp.cumsum(onehot, axis=0) - onehot
    position = jnp.sum(earlier * onehot, axis=1)
    capacity = 2 * groups // dp_count
    slot_index = dests * capacity + position
    scatter_table = (
        slot_index[None, :] == jnp.arange(dp_count * capacity, dtype=jnp.int32)[:, None]
    ).astype(jnp.bfloat16)
    outgoing = jnp.dot(scatter_table, projected, preferred_element_type=jnp.float32).astype(
        jnp.bfloat16
    )
    outgoing = outgoing.reshape(dp_count, capacity, -1)
    arrived = lax.all_to_all(outgoing, "dp", split_axis=0, concat_axis=0, tiled=True)
    return arrived.reshape(dp_count * capacity, -1)


def solution(mesh):
    return jax.shard_map(
        shards,
        mesh=mesh,
        in_specs=(
            P(("dp", "tensor"), None),
            P(),
            P(),
            P(None, "tensor", None),
            P("tensor", None, None),
            P(),
            P(),
            P("dp", "tensor"),
            P("tensor"),
            P("dp", None),
            P("dp", None),
        ),
        out_specs=P("dp", "tensor"),
        check_vma=False,
    )
```

profile of v0, /device:TPU:8, one launch (start us, length us, event | category | flops | bytes accessed | tf_op | source)
XLA Modules:
  0.0 273.7 jit_solution(15908829058235544437)
XLA Ops:
  7.4 0.7 all-gather.3.cloned.1.call-update
  8.1 0.7 slice_bitcast_fusion.1
  9.2 0.8 broadcast_in_dim.25
  10.1 0.7 broadcast_compare_fusion.1
  10.8 38.3 %all-gather.3.cloned.1.call-done = bf16[1024,1408]{1,0:T(8,128)(2,1)} async-done(((bf16[128,1408]{1,0:T(8,128)(2,1)}), bf16[1024,1408]{1,0:T(8,128)(2,1)}) %all-gather.3.cloned.1.call-update) | async-done | bytes 2883600 | tf_op jit(solution)/shard_map/all_gather | solution.py:59
  49.1 2.4 convert_reduce_fusion
  51.7 0.9 fusion.6
  52.7 3.1 %fusion.31 = bf16[1024,528]{0,1:T(8,128)(2,1)} fusion(bf16[1408,528]{0,1:T(8,128)(2,1)S(1)} %bitcast.40, bf16[1024,1408]{1,0:T(8,128)(2,1)S(1)} %copy-done.1, f32[1408]{0:T(1024)S(1)} %copy-done.8, f32[1408]{0:T(1024)S(1)} %copy-done.9, f32[1024]{0:T(1024)S(1)} %add_rsqrt_fusion.1, f32[1024]{0:T(1024)S(1)} %broadcast_multiply_fusion.1), kind=kOutput, calls=%fused_computation.42 | convolution fusion | flops 1531723776 | bytes 5471232 | tf_op jit(solution)/shard_map/dot_general | solution.py:63
  55.8 4.8 %fusion.90 = (f32[2,512]{1,0:T(2,128)S(1)}, f32[2,512,1024]{2,1,0:T(8,128)}) fusion(pred[512,1024]{1,0:T(8,128)(4,1)S(1)} %get-tuple-element.5, bf16[1024,2,264]{0,2,1:T(8,128)(2,1)} %bitcast.47), kind=kOutput, calls=%fused_computation.94 | convolution fusion | flops 188744704 | bytes 5263360 | tf_op jit(solution)/shard_map/sub | solution.py:38
  60.6 4.9 %fusion.81 = (f32[2,512]{1,0:T(2,128)S(1)}, f32[2,512,1024]{2,1,0:T(8,128)}) fusion(pred[512,1024]{1,0:T(8,128)(4,1)S(1)} %get-tuple-element.6, bf16[1024,2,264]{0,2,1:T(8,128)(2,1)} %bitcast.48), kind=kOutput, calls=%fused_computation.93 | convolution fusion | flops 188744704 | bytes 5263360 | tf_op jit(solution)/shard_map/sub | solution.py:38
  65.4 3.2 %fusion.37 = bf16[512,2,88]{0,2,1:T(8,128)(2,1)S(1)} fusion(f32[2,512,1024]{2,1,0:T(8,128)} %get-tuple-element.12, f32[2,512]{1,0:T(2,128)S(1)} %get-tuple-element.11, bf16[1024,2,264]{0,2,1:T(8,128)(2,1)S(1)} %bitcast.49), kind=kOutput, calls=%fused_computation.48 | convolution fusion | flops 186736640 | bytes 4739072 | tf_op jit(solution)/shard_map/hqk,khd->qhd/dot_general | solution.py:40
  68.9 0.9 fusion.38
  69.9 2.7 bitcast_convert_fusion
  73.2 0.6 reduce-window.6
  74.2 83.9 %all-reduce.2.cloned.1.call-done = bf16[1024,1408]{1,0:T(8,128)(2,1)} async-done(((bf16[1024,1408]{1,0:T(8,128)(2,1)}), bf16[1024,1408]{1,0:T(8,128)(2,1)}) %all-reduce.2.cloned.1.call-update) | async-done | bytes 2883600 | tf_op jit(solution)/shard_map/psum | solution.py:70
  158.0 3.6 %convert_reduce_fusion.1 = f32[1024]{0:T(1024)S(1)} fusion(bf16[1024,1408]{1,0:T(8,128)(2,1)} %all-reduce.2.cloned.1.call-done, bf16[1024,1408]{1,0:T(8,128)(2,1)} %all-gather.3.cloned.1.call-done), kind=kLoop, calls=%fused_computation.6 | loop fusion | flops 8649728 | bytes 5771264 | tf_op jit(solution)/shard_map/reduce_sum | solution.py:9
  161.7 0.7 copy-done.3
  162.4 1.2 fusion.10
  163.7 2.9 %fusion.13 = bf16[1024,1408]{1,0:T(8,128)(2,1)} fusion(f32[1408]{0:T(1024)S(1)} %copy-done.6, f32[1408]{0:T(1024)S(1)} %copy-done.7, f32[1024]{0:T(1024)S(1)} %add_rsqrt_fusion, f32[1024]{0:T(1024)S(1)} %broadcast_multiply_fusion, bf16[1024,1408]{1,0:T(8,128)(2,1)S(1)} %copy-done.3, bf16[1024,1408]{1,0:T(8,128)(2,1)S(1)} %copy-done.2), kind=kLoop, calls=%fused_computation.18 | loop fusion | flops 14417920 | bytes 8670208 | tf_op jit(solution)/shard_map/convert_element_type | solution.py:75
  166.5 5.7 %reshape.149 = bf16[256,5632]{1,0:T(8,128)(2,1)} reshape(bf16[1024,1408]{1,0:T(8,128)(2,1)} %fusion.13) | data formatting | bytes 5767168 | tf_op jit(solution)/shard_map/reshape | solution.py:77
  172.2 54.6 %all-gather.5.cloned.1.call-done = bf16[5632,448]{1,0:T(8,128)(2,1)} async-done(((bf16[88,448]{1,0:T(8,128)(2,1)}), bf16[5632,448]{1,0:T(8,128)(2,1)}) %all-gather.5.cloned.1.call-update) | async-done | bytes 5046288 | tf_op jit(solution)/shard_map/all_gather | solution.py:79
  226.8 5.5 %convolution_convert_fusion = bf16[512,448]{0,1:T(8,128)(2,1)S(1)} fusion(bf16[256,5632]{1,0:T(8,128)(2,1)} %reshape.149, bf16[5632,448]{1,0:T(8,128)(2,1)} %all-gather.5.cloned.1.call-done, f32[448]{0:T(512)S(1)} %copy-done.10, s32[256]{0:T(256)S(1)} %multiply_add_fusion), kind=kOutput, calls=%fused_computation.43 | convolution fusion | flops 1409875968 | bytes 8391424 | tf_op jit(solution)/shard_map/dot_general | solution.py:91
  232.4 32.8 %all_to_all.5 = bf16[64,8,448]{2,1,0:T(8,128)(2,1)S(1)} all-to-all(bf16[64,8,448]{2,1,0:T(8,128)(2,1)S(1)} %bitcast.41), channel_id=1, replica_groups=mesh['dp'=64,'tensor'=8] {'dp'}, dimensions={0} | all-to-all | bytes 917504 | tf_op jit(solution)/shard_map/all_to_all | solution.py:95
  265.3 1.0 copy.14
  (46 shorter events, 2.4 us)
Async XLA Ops:
  7.4 45.3 %copy-start = (bf16[1408,2,264]{0,2,1:T(8,128)(2,1)S(1)}, bf16[1408,2,264]{0,2,1:T(8,128)(2,1)}, u32[]{:S(2)}) copy-start(bf16[1408,2,264]{0,2,1:T(8,128)(2,1)} %param.14) | copy-start | bytes 4460548
  7.4 45.3 %copy-start.9 = (f32[1408]{0:T(1024)S(1)}, f32[1408]{0:T(1024)}, u32[]{:S(2)}) copy-start(f32[1408]{0:T(1024)} %param.12) | copy-start | bytes 16900
  7.4 45.3 %copy-start.8 = (f32[1408]{0:T(1024)S(1)}, f32[1408]{0:T(1024)}, u32[]{:S(2)}) copy-start(f32[1408]{0:T(1024)} %param.13) | copy-start | bytes 16900
  7.4 41.7 %all-gather.3.cloned.1.call-start = ((), (), s32[]{:S(2)}) async-start(), calls=%async_computation.1 | async-start | bytes 3244032 | tf_op jit(solution)/shard_map/all_gather | solution.py:59
  8.1 149.9 %all-reduce.2.cloned.1.call-start = ((), (), s32[]{:S(2)}) async-start(), calls=%async_computation.2 | async-start | bytes 5767168 | tf_op jit(solution)/shard_map/psum | solution.py:70
  49.1 2.7 copy-start.1
  60.6 4.9 %copy-start.11 = (bf16[1024,528]{0,1:T(8,128)(2,1)S(1)}, bf16[1024,528]{0,1:T(8,128)(2,1)}, u32[]{:S(2)}) copy-start(bf16[1024,528]{0,1:T(8,128)(2,1)} %fusion.31) | copy-start | bytes 3244036
  65.4 3.4 %copy-start.12 = (f32[2,512,1024]{2,1,0:T(8,128)S(1)}, f32[2,512,1024]{2,1,0:T(8,128)}, u32[]{:S(2)}) copy-start(f32[2,512,1024]{2,1,0:T(8,128)} %get-tuple-element.10) | copy-start | bytes 12582916
  68.9 1.0 copy-start.4
  69.9 3.3 %copy-start.5 = (s32[256,1]{0,1:T(1,128)S(1)}, s32[256,1]{0,1:T(1,128)}, u32[]{:S(2)}) copy-start(s32[256,1]{0,1:T(1,128)} %param.21) | copy-start | bytes 3076
  72.6 154.1 %all-gather.5.cloned.1.call-start = ((), (), s32[]{:S(2)}) async-start(), calls=%async_computation.3 | async-start | bytes 5857280 | tf_op jit(solution)/shard_map/all_gather | solution.py:79
  158.0 3.7 %copy-start.2 = (bf16[1024,1408]{1,0:T(8,128)(2,1)S(1)}, bf16[1024,1408]{1,0:T(8,128)(2,1)}, u32[]{:S(2)}) copy-start(bf16[1024,1408]{1,0:T(8,128)(2,1)} %all-gather.3.cloned.1.call-done) | copy-start | bytes 8650756
  158.0 4.4 %copy-start.3 = (bf16[1024,1408]{1,0:T(8,128)(2,1)S(1)}, bf16[1024,1408]{1,0:T(8,128)(2,1)}, u32[]{:S(2)}) copy-start(bf16[1024,1408]{1,0:T(8,128)(2,1)} %all-reduce.2.cloned.1.call-done) | copy-start | bytes 8650756
  161.7 2.0 copy-start.6
  161.7 2.0 copy-start.7
  166.5 60.2 %copy-start.10 = (f32[448]{0:T(512)S(1)}, f32[448]{0:T(512)}, u32[]{:S(2)}) copy-start(f32[448]{0:T(512)} %param.19) | copy-start | bytes 5380
Sparse Core Ops, SparseCore 0:
  10.3 38.6 all-gather.2
  72.7 85.2 all-reduce.1
Sparse Core Ops, SparseCore 1:
  76.0 150.7 all-gather.4
where the time goes:
time: 274 us
  waiting for transfers between devices  178 us (65%)
  blocking collectives  32.8 us (12%)
  matrix products  24.9 us (9%)
  between operations  15 us (5%)
  other arithmetic  12.5 us (5%)
  local copies, waits for them, and re-layouts  10.4 us (4%)
    psum x1, waiting for transfers between devices, shards(): lax.psum(jnp.dot(context, out_flat, preferred_element_type=jnp.float32).a...  83.9 us
    all_gather x1, waiting for transfers between devices, shards(): lax.all_gather(w_proj, 'dp', axis=0, tiled=True)  54.6 us
    all_gather x1, waiting for transfers between devices, shards(): gathered = lax.all_gather(tokens, 'tensor', axis=0, tiled=True)  38.3 us
    all_to_all x1, blocking collectives, shards(): lax.all_to_all(outgoing, 'dp', split_axis=0, concat_axis=0, tiled=True)  32.8 us
    sub x2, matrix products, attend(): exponent = jnp.exp(scores - row_max)  9.63 us
    reduce_sum x2, other arithmetic, layer_norm(): average = jnp.mean(wide, axis=-1, keepdims=True)  6.05 us
    reshape x1, local copies, waits for them, and re-layouts, shards(): merged = normed_all.reshape(groups, -1)  5.67 us
  transfers between devices with their start and end apart: 3, of which 3 were waited for; matrix products, arithmetic and copies ran while one was open for 6% of the time, Pallas kernels for 0%

commit v1 on v0

--- a/solution.py
+++ b/solution.py
@@ -67,9 +67,12 @@
     token_segs = jnp.repeat(segments[0], 4)
     context = attend(heads_qkv, token_segs).reshape(row_count, -1)
     out_flat = w_out.reshape(-1, w_out.shape[2])
-    attn_all = lax.psum(
-        jnp.dot(context, out_flat, preferred_element_type=jnp.float32).astype(jnp.bfloat16),
-        "tensor",
+    attn_all = jnp.sum(
+        lax.all_gather(
+            jnp.dot(context, out_flat, preferred_element_type=jnp.float32).astype(jnp.bfloat16),
+            "tensor",
+        ),
+        axis=0,
     ).astype(jnp.float32)
     hidden = (gathered.astype(jnp.float32) + attn_all).astype(jnp.bfloat16)
     normed_all = layer_norm(hidden, ln2_gain, ln2_shift).astype(jnp.bfloat16)

time: 274 us -> 392 us (1.43)
  the two profiles are of different devices: /device:TPU:8 before, /device:TPU:2 now
where the time goes in v1:
time: 392 us
  waiting for transfers between devices  284 us (72%)
  blocking collectives  32.8 us (8%)
  other arithmetic  26.6 us (7%)
  matrix products  24.7 us (6%)
  between operations  13.3 us (3%)
  local copies, waits for them, and re-layouts  10.4 us (3%)
    all_gather x1, waiting for transfers between devices, shards(): lax.all_gather(w_proj, 'dp', axis=0, tiled=True)  126 us
    all_gather x1, waiting for transfers between devices, shards(): lax.all_gather(jnp.dot(context, out_flat, preferred_element_type=jnp.floa...  119 us
    all_gather x1, waiting for transfers between devices, shards(): gathered = lax.all_gather(tokens, 'tensor', axis=0, tiled=True)  37.6 us
    all_to_all x1, blocking collectives, shards(): lax.all_to_all(outgoing, 'dp', split_axis=0, concat_axis=0, tiled=True)  32.8 us
    reduce_sum x1, other arithmetic, shards(): jnp.sum(lax.all_gather(jnp.dot(context, out_flat, preferred_element_type=...  14.1 us
    sub x2, matrix products, attend(): exponent = jnp.exp(scores - row_max)  9.42 us
  transfers between devices with their start and end apart: 3, of which 3 were waited for; matrix products, arithmetic and copies ran while one was open for 8% of the time, Pallas kernels for 0%

profile of v1, /device:TPU:2, one launch (start us, length us, event | category | flops | bytes accessed | tf_op | source)
XLA Modules:
  0.0 391.7 jit_solution(11606742349018595705)
XLA Ops:
  6.5 0.7 all-gather.5.cloned.1.call-update
  7.3 0.7 slice_bitcast_fusion.1
  8.4 0.8 broadcast_in_dim.25
  9.3 0.7 broadcast_compare_fusion.1
  9.9 37.6 %all-gather.5.cloned.1.call-done = bf16[1024,1408]{1,0:T(8,128)(2,1)} async-done(((bf16[128,1408]{1,0:T(8,128)(2,1)}), bf16[1024,1408]{1,0:T(8,128)(2,1)}) %all-gather.5.cloned.1.call-update) | async-done | bytes 2883600 | tf_op jit(solution)/shard_map/all_gather | solution.py:59
  47.6 2.4 convert_reduce_fusion
  50.2 0.9 fusion.6
  51.2 3.2 fusion.31
  54.4 4.7 %fusion.90 = (f32[2,512]{1,0:T(2,128)S(1)}, f32[2,512,1024]{2,1,0:T(8,128)}) fusion(pred[512,1024]{1,0:T(8,128)(4,1)S(1)} %get-tuple-element.5, bf16[1024,2,264]{0,2,1:T(8,128)(2,1)} %bitcast.49), kind=kOutput, calls=%fused_computation.94 | convolution fusion | flops 188744704 | bytes 5263360 | tf_op jit(solution)/shard_map/sub | solution.py:38
  59.1 4.7 %fusion.81 = (f32[2,512]{1,0:T(2,128)S(1)}, f32[2,512,1024]{2,1,0:T(8,128)}) fusion(pred[512,1024]{1,0:T(8,128)(4,1)S(1)} %get-tuple-element.6, bf16[1024,2,264]{0,2,1:T(8,128)(2,1)} %bitcast.50), kind=kOutput, calls=%fused_computation.93 | convolution fusion | flops 188744704 | bytes 5263360 | tf_op jit(solution)/shard_map/sub | solution.py:38
  63.8 3.2 fusion.37
  67.2 0.9 fusion.38
  68.3 2.6 bitcast_convert_fusion
  72.6 118.8 %all-gather.9.cloned.1.call-done = bf16[8192,1408]{1,0:T(8,128)(2,1)} async-done(((bf16[1024,1408]{1,0:T(8,128)(2,1)}), bf16[8192,1408]{1,0:T(8,128)(2,1)}) %all-gather.9.cloned.1.call-update) | async-done | bytes 23068688 | tf_op jit(solution)/shard_map/all_gather | solution.py:71
  191.4 14.1 %reduce_sum.80 = bf16[1024,1408]{1,0:T(8,128)(2,1)} reduce(bf16[8,1024,1408]{2,1,0:T(8,128)(2,1)} %bitcast.42, bf16[]{:T(256)} %constant.23.clone.1), dimensions={0}, to_apply=%region_9.10 | reduce | flops 10092544 | bytes 25952258 | tf_op jit(solution)/shard_map/reduce_sum | solution.py:70
  205.5 3.6 convert_reduce_fusion.1
  209.2 0.7 copy-done.3
  209.9 1.2 fusion.10
  211.1 2.9 fusion.13
  214.0 5.7 %reshape.149 = bf16[256,5632]{1,0:T(8,128)(2,1)} reshape(bf16[1024,1408]{1,0:T(8,128)(2,1)} %fusion.13) | data formatting | bytes 5767168 | tf_op jit(solution)/shard_map/reshape | solution.py:80
  219.7 126.1 %all-gather.7.cloned.1.call-done = bf16[5632,448]{1,0:T(8,128)(2,1)} async-done(((bf16[88,448]{1,0:T(8,128)(2,1)}), bf16[5632,448]{1,0:T(8,128)(2,1)}) %all-gather.7.cloned.1.call-update) | async-done | bytes 5046288 | tf_op jit(solution)/shard_map/all_gather | solution.py:82
  345.8 5.5 %convolution_convert_fusion = bf16[512,448]{0,1:T(8,128)(2,1)S(1)} fusion(bf16[256,5632]{1,0:T(8,128)(2,1)} %reshape.149, bf16[5632,448]{1,0:T(8,128)(2,1)} %all-gather.7.cloned.1.call-done, f32[448]{0:T(512)S(1)} %copy-done.10, s32[256]{0:T(256)S(1)} %multiply_add_fusion), kind=kOutput, calls=%fused_computation.43 | convolution fusion | flops 1409875968 | bytes 8391424 | tf_op jit(solution)/shard_map/dot_general | solution.py:94
  351.4 32.8 %all_to_all.5 = bf16[64,8,448]{2,1,0:T(8,128)(2,1)S(1)} all-to-all(bf16[64,8,448]{2,1,0:T(8,128)(2,1)S(1)} %bitcast.43), channel_id=1, replica_groups=mesh['dp'=64,'tensor'=8] {'dp'}, dimensions={0} | all-to-all | bytes 917504 | tf_op jit(solution)/shard_map/all_to_all | solution.py:98
  384.2 1.0 copy.14
  (47 shorter events, 3.2 us)
Async XLA Ops:
  6.5 44.6 %copy-start = (bf16[1408,2,264]{0,2,1:T(8,128)(2,1)S(1)}, bf16[1408,2,264]{0,2,1:T(8,128)(2,1)}, u32[]{:S(2)}) copy-start(bf16[1408,2,264]{0,2,1:T(8,128)(2,1)} %param.14) | copy-start | bytes 4460548
  6.5 44.6 %copy-start.9 = (f32[1408]{0:T(1024)S(1)}, f32[1408]{0:T(1024)}, u32[]{:S(2)}) copy-start(f32[1408]{0:T(1024)} %param.12) | copy-start | bytes 16900
  6.5 44.6 %copy-start.8 = (f32[1408]{0:T(1024)S(1)}, f32[1408]{0:T(1024)}, u32[]{:S(2)}) copy-start(f32[1408]{0:T(1024)} %param.13) | copy-start | bytes 16900
  6.5 41.0 %all-gather.5.cloned.1.call-start = ((), (), s32[]{:S(2)}) async-start(), calls=%async_computation.1 | async-start | bytes 3244032 | tf_op jit(solution)/shard_map/all_gather | solution.py:59
  7.3 184.1 %all-gather.9.cloned.1.call-start = ((), (), s32[]{:S(2)}) async-start(), calls=%async_computation.3 | async-start | bytes 25952256 | tf_op jit(solution)/shard_map/all_gather | solution.py:71
  47.6 2.7 copy-start.1
  59.1 4.7 %copy-start.11 = (bf16[1024,528]{0,1:T(8,128)(2,1)S(1)}, bf16[1024,528]{0,1:T(8,128)(2,1)}, u32[]{:S(2)}) copy-start(bf16[1024,528]{0,1:T(8,128)(2,1)} %fusion.31) | copy-start | bytes 3244036
  63.8 3.4 copy-start.12
  67.2 1.0 copy-start.4
  68.3 3.3 copy-start.5
  70.9 274.9 %all-gather.7.cloned.1.call-start = ((), (), s32[]{:S(2)}) async-start(), calls=%async_computation.2 | async-start | bytes 5857280 | tf_op jit(solution)/shard_map/all_gather | solution.py:82
  205.5 3.7 copy-start.2
  205.5 4.4 %copy-start.3 = (bf16[1024,1408]{1,0:T(8,128)(2,1)S(1)}, bf16[1024,1408]{1,0:T(8,128)(2,1)}, u32[]{:S(2)}) copy-start(bf16[1024,1408]{1,0:T(8,128)(2,1)} %reduce_sum.80) | copy-start | bytes 8650756
  209.1 2.0 copy-start.6
  209.2 2.0 copy-start.7
  214.0 131.7 %copy-start.10 = (f32[448]{0:T(512)S(1)}, f32[448]{0:T(512)}, u32[]{:S(2)}) copy-start(f32[448]{0:T(512)} %param.19) | copy-start | bytes 5380
Sparse Core Ops, SparseCore 0:
  9.5 38.0 all-gather.4
  71.0 120.3 all-gather.8
  194.3 151.3 all-gather.6
